TPU v7x, 32 devices: a whole 2x2x4 slice. The times are simulated.
32 devices in a mesh: seq: 8 (over z, y), head: 2 (over x), cfg: 2 (over core).
Axes of the slice: x: 2, y: 2, z: 4, core: 2. Of those that a mesh axis runs over, the one named last changes fastest.
Arguments:
- queries: bfloat16 [6144, 5120], P(('cfg', 'seq'), 'head'), parts along dimension 0, may hold values from -16 to 16
- fresh_key: bfloat16 [6144, 5120], P(('cfg', 'seq'), 'head'), parts along dimension 0, may hold values from -16 to 16
- fresh_value: bfloat16 [6144, 5120], P(('cfg', 'seq'), 'head'), parts along dimension 0, may hold values from -6 to 6
- stale_key: bfloat16 [6144, 5120], P(('cfg', 'seq'), 'head'), parts along dimension 0, may hold values from -6 to 6
- stale_value: bfloat16 [6144, 5120], P(('cfg', 'seq'), 'head'), parts along dimension 0, may hold values from -6 to 6
- slot_tiles: int32 [48], P('cfg'), parts along dimension 0, may hold values from 0 to 23, as said below
- refresh: int32 [48], P('cfg'), parts along dimension 0, may hold values from 0 to 1, as said below
- stale_reads: int32 [16, 24], P('cfg'), parts along dimension 0, may hold values from 0 to 1, as said below
- out_weight: bfloat16 [5120, 5120], P('head'), may hold values from -6 to 6
Outputs:
- mixed: bfloat16 [6144, 5120], P(('cfg', 'seq', 'head')), parts along dimension 0
There are 2 independent parts, one for each index of `cfg`. A program takes and returns all parts, laid end to end along the dimension named above; an argument that names none is the same for every part. Nothing has to cross between parts.
Inputs may be any that keep to these rules, and one draw needn't show every extreme that they name: `slot_tiles`: A permutation of the 24 tiles. Cache slot i lies on index i // 3 of seq; the slots of every index of seq hold at least one tile that is not refreshed. `refresh`: tile t belongs to index t // 3 of seq. Every index of seq owns between 1 and 2 refreshed tiles; some index owns exactly 1 and some exactly 2. `stale_reads`: only tiles that are not refreshed are read. A reader reads at most one tile among the slots of any one index of seq; some reader reads one tile from the slots of every index.
All inputs are finite; a program needn't handle non-finite values.
Results may differ from a plain program's by a relative error of at most 0.019.
Values may be sent and summed in bfloat16 or wider, within the bound.
No kernel may reach another device: no remote copies, remote signals or barrier semaphores. Data moves between devices by JAX's collectives and lax.ppermute only.
A program may use at most 256 MiB of HBM per device.

v0:
```python
import jax
import jax.numpy as jnp
from jax import lax
from jax.experimental import pallas as pl
from jax.experimental.pallas import tpu as pltpu
from jax.sharding import PartitionSpec as P

HD = 128
TILE = 128


NEG = -1e30


def _scores(q_ref, kf0_ref, kf1_ref, ks_ref, j, second, valid):
    sl = slice(j * HD, (j + 1) * HD)
    qj = q_ref[0, :, sl]
    dims = (((1,), (1,)), ((), ()))
    scale = HD ** -0.5
    s0 = lax.dot_general(kf0_ref[0, :, sl], qj, dims, preferred_element_type=jnp.float32) * scale
    s1 = lax.dot_general(kf1_ref[0, :, sl], qj, dims, preferred_element_type=jnp.float32) * scale
    s2 = lax.dot_general(ks_ref[0, :, sl], qj, dims, preferred_element_type=jnp.float32) * scale
    s1 = jnp.where(second > 0, s1, NEG)
    s2 = jnp.where(valid > 0, s2, NEG)
    return s0, s1, s2


def part_kernel(
    fsel_ref, rs_ref, q_ref, kf0_ref, kf1_ref, ks_ref, vf0_ref, vf1_ref, vs_ref, acc_ref, st_ref
):
    heads_part = q_ref.shape[1] // HD
    second = fsel_ref[2]
    valid = rs_ref[1]
    tn = (((0,), (0,)), ((), ()))
    dims = (((1,), (1,)), ((), ()))
    scale = HD ** -0.5
    def head(j, carry):
        c = pl.multiple_of(j * HD, HD)
        sl = pl.ds(c, HD)
        qj = q_ref[:, sl]
        s0 = lax.dot_general(kf0_ref[0, :, sl], qj, dims, preferred_element_type=jnp.float32) * scale
        s1 = lax.dot_general(kf1_ref[0, :, sl], qj, dims, preferred_element_type=jnp.float32) * scale
        s2 = lax.dot_general(ks_ref[0, :, sl], qj, dims, preferred_element_type=jnp.float32) * scale
        s1 = jnp.where(second > 0, s1, NEG)
        s2 = jnp.where(valid > 0, s2, NEG)
        top = jnp.maximum(
            jnp.maximum(jnp.max(s0, axis=0, keepdims=True), jnp.max(s1, axis=0, keepdims=True)),
            jnp.max(s2, axis=0, keepdims=True),
        )
        w0 = jnp.exp(s0 - top)
        w1 = jnp.exp(s1 - top)
        w2 = jnp.exp(s2 - top)
        total = (
            jnp.sum(w0, axis=0, keepdims=True)
            + jnp.sum(w1, axis=0, keepdims=True)
            + jnp.sum(w2, axis=0, keepdims=True)
        )
        summed = (
            lax.dot_general(vf0_ref[0, :, sl], w0.astype(jnp.bfloat16), tn, preferred_element_type=jnp.float32)
            + lax.dot_general(vf1_ref[0, :, sl], w1.astype(jnp.bfloat16), tn, preferred_element_type=jnp.float32)
            + lax.dot_general(vs_ref[0, :, sl], w2.astype(jnp.bfloat16), tn, preferred_element_type=jnp.float32)
        )
        acc_ref[sl, :] = summed.astype(acc_ref.dtype)
        st_ref[0, pl.ds(j, 1), :] = top
        st_ref[1, pl.ds(j, 1), :] = total
        return carry

    lax.fori_loop(0, heads_part, head, 0)


def attend_part(q, fsel, rs, fk3, fv3, sk3, sv3):
    tokens, width = q.shape
    heads_part = width // HD
    full = pl.BlockSpec((tokens, width), lambda i, f, r: (0, 0))
    f0 = pl.BlockSpec((1, TILE, width), lambda i, f, r: (f[0], 0, 0))
    f1 = pl.BlockSpec((1, TILE, width), lambda i, f, r: (f[1], 0, 0))
    st = pl.BlockSpec((1, TILE, width), lambda i, f, r: (r[0], 0, 0))
    return pl.pallas_call(
        part_kernel,
        grid_spec=pltpu.PrefetchScalarGridSpec(
            num_scalar_prefetch=2,
            grid=(1,),
            in_specs=[full, f0, f1, st, f0, f1, st],
            out_specs=[
                pl.BlockSpec((width, tokens), lambda i, f, r: (0, 0)),
                pl.BlockSpec((2, heads_part, tokens), lambda i, f, r: (0, 0, 0)),
            ],
        ),
        out_shape=[
            jax.ShapeDtypeStruct((width, tokens), jnp.bfloat16),
            jax.ShapeDtypeStruct((2, heads_part, tokens), jnp.float32),
        ],
        compiler_params=pltpu.CompilerParams(dimension_semantics=("arbitrary",)),
    )(fsel, rs, q, fk3, fk3, sk3, fv3, fv3, sv3)


def ring_order(n):
    if n == 8:
        return [0, 2, 4, 6, 7, 5, 3, 1]
    return list(range(n))


def combine(run, mine):
    acc_r, stat_r = run
    acc_o, stat_o = mine
    top = jnp.maximum(stat_r[0], stat_o[0])
    f_r = jnp.exp(stat_r[0] - top)
    f_o = jnp.exp(stat_o[0] - top)
    total = stat_r[1] * f_r + stat_o[1] * f_o
    acc = acc_r.astype(jnp.float32) * jnp.repeat(f_r, HD, axis=0) + acc_o.astype(
        jnp.float32
    ) * jnp.repeat(f_o, HD, axis=0)
    return acc, jnp.stack([top, total])


def on_device(
    queries,
    fresh_key,
    fresh_value,
    stale_key,
    stale_value,
    slot_tiles,
    refresh,
    stale_reads,
    out_weight,
):
    tokens_here = queries.shape[0]
    width_here = queries.shape[1]
    heads_here = width_here // HD
    tile_dev = tokens_here // TILE
    readers = stale_reads.shape[0]
    me = lax.axis_index("seq")

    my_refresh = lax.dynamic_slice_in_dim(refresh, me * tile_dev, tile_dev, 0)
    first = jnp.argmax(my_refresh).astype(jnp.int32)
    last = (tile_dev - 1 - jnp.argmax(my_refresh[::-1])).astype(jnp.int32)
    second = (jnp.sum(my_refresh) >= 2).astype(jnp.int32)
    fsel = jnp.stack([first, last, second])

    my_slots = lax.dynamic_slice_in_dim(slot_tiles, me * tile_dev, tile_dev, 0)
    wanted = jnp.take(stale_reads, my_slots, axis=1)
    sidx = jnp.argmax(wanted, axis=1).astype(jnp.int32)
    sval = jnp.max(wanted, axis=1).astype(jnp.int32)

    fk3 = fresh_key.reshape(tile_dev, TILE, width_here)
    fv3 = fresh_value.reshape(tile_dev, TILE, width_here)
    sk3 = stale_key.reshape(tile_dev, TILE, width_here)
    sv3 = stale_value.reshape(tile_dev, TILE, width_here)

    ring = ring_order(readers)
    place = [0] * readers
    for i, d in enumerate(ring):
        place[d] = i
    pos = jnp.array(place, jnp.int32)[me]
    ring_arr = jnp.array(ring, jnp.int32)
    forward = [(ring[i], ring[(i + 1) % readers]) for i in range(readers)]
    backward = [(ring[i], ring[(i - 1) % readers]) for i in range(readers)]
    cut = (heads_here // 2) * HD
    halves = []
    for lo, hi in ((0, cut), (cut, width_here)):
        halves.append(
            (queries[:, lo:hi], fk3[:, :, lo:hi], fv3[:, :, lo:hi], sk3[:, :, lo:hi], sv3[:, :, lo:hi])
        )

    def own(half, q, reader):
        _, k3, v3, s3, t3 = halves[half]
        rs = jnp.stack([sidx[reader], sval[reader]])
        return attend_part(q, fsel, rs, k3, v3, s3, t3)

    moving = [halves[0][0], halves[1][0]]
    run = [None, None]
    perms = (forward, backward)
    for t in range(1, readers):
        got_q = [lax.ppermute(moving[h], "seq", perms[h]) for h in range(2)]
        got_run = [None, None] if t == 1 else [lax.ppermute(run[h], "seq", perms[h]) for h in range(2)]
        readers_t = (ring_arr[(pos - t + readers) % readers], ring_arr[(pos + t) % readers])
        for h in range(2):
            mine = own(h, got_q[h], readers_t[h])
            run[h] = mine if t == 1 else combine(got_run[h], mine)
            run[h] = (run[h][0].astype(jnp.bfloat16), run[h][1])
        moving = got_q
    got_run = [lax.ppermute(run[h], "seq", perms[h]) for h in range(2)]
    run_f = combine(got_run[0], own(0, halves[0][0], me))
    run_b = combine(got_run[1], own(1, halves[1][0], me))
    acc = jnp.concatenate([run_f[0], run_b[0]], axis=0)
    total = jnp.concatenate([run_f[1][1], run_b[1][1]], axis=0)
    attended = (acc / jnp.repeat(total, HD, axis=0)).astype(jnp.bfloat16)
    mixed = lax.dot_general(
        attended, out_weight, (((0,), (0,)), ((), ())), preferred_element_type=jnp.float32
    )
    return lax.psum_scatter(mixed.astype(jnp.bfloat16), "head", scatter_dimension=0, tiled=True)


def solution(mesh):
    return jax.shard_map(
        on_device,
        mesh=mesh,
        in_specs=(
            P(("cfg", "seq"), "head"),
            P(("cfg", "seq"), "head"),
            P(("cfg", "seq"), "head"),
            P(("cfg", "seq"), "head"),
            P(("cfg", "seq"), "head"),
            P("cfg"),
            P("cfg"),
            P("cfg", None),
            P("head", None),
        ),
        out_specs=P(("cfg", "seq", "head"), None),
        check_vma=False,
    )
```

profile of v0, /device:TPU:0, one launch (start us, length us, event | category | flops | bytes accessed | tf_op | source)
XLA Modules:
  0.0 443.1 jit_solution(10438289390329180474)
XLA Ops:
  8.3 3.0 collective-permute-start.21
  34.8 4.2 fusion.78
  47.4 9.4 %shard_map.117 = (bf16[1280,384]{1,0:T(8,128)(2,1)}, f32[2,10,384]{2,1,0:T(8,128)}) custom-call(s32[3]{0:T(128)} %pad_add_fusion.fsel_ref, s32[2]{0:T(128)} %pad_add_fusion.7.rs_ref, bf16[384,1280]{1,0:T(8,128)(2,1)} %collective-permute-done.21.q_ref, bf16[3,128,1280]{2,1,0:T(8,128)(2,1)} %get-tuple-element.176.kf0_ref.kf1_ref, ...), custom_call_target="tpu_custom_call" | custom-call | tf_op jit(solution)/shard_map/pallas_call | solution.py:78
  62.7 9.6 %shard_map.109 = (bf16[1280,384]{1,0:T(8,128)(2,1)}, f32[2,10,384]{2,1,0:T(8,128)}) custom-call(s32[3]{0:T(128)} %pad_add_fusion.fsel_ref, s32[2]{0:T(128)} %pad_add_fusion.1.rs_ref, bf16[384,1280]{1,0:T(8,128)(2,1)} %copy-done.4, bf16[3,128,1280]{2,1,0:T(8,128)(2,1)} %get-tuple-element.177.kf0_ref.kf1_ref, ...), custom_call_target="tpu_custom_call" | custom-call | tf_op jit(solution)/shard_map/pallas_call | solution.py:78
  83.4 9.4 %shard_map.124 = (bf16[1280,384]{1,0:T(8,128)(2,1)}, f32[2,10,384]{2,1,0:T(8,128)}) custom-call(s32[3]{0:T(128)} %pad_add_fusion.fsel_ref, s32[2]{0:T(128)} %pad_add_fusion.8.rs_ref, bf16[384,1280]{1,0:T(8,128)(2,1)} %copy-done.1, bf16[3,128,1280]{2,1,0:T(8,128)(2,1)} %get-tuple-element.176.kf0_ref.kf1_ref, ...), custom_call_target="tpu_custom_call" | custom-call | tf_op jit(solution)/shard_map/pallas_call | solution.py:78
  92.8 9.5 %shard_map.116 = (bf16[1280,384]{1,0:T(8,128)(2,1)}, f32[2,10,384]{2,1,0:T(8,128)}) custom-call(s32[3]{0:T(128)} %pad_add_fusion.fsel_ref, s32[2]{0:T(128)} %pad_add_fusion.8.rs_ref, bf16[384,1280]{1,0:T(8,128)(2,1)} %copy-done, bf16[3,128,1280]{2,1,0:T(8,128)(2,1)} %get-tuple-element.177.kf0_ref.kf1_ref, ...), custom_call_target="tpu_custom_call" | custom-call | tf_op jit(solution)/shard_map/pallas_call | solution.py:78
  103.3 9.4 %shard_map.118 = (bf16[1280,384]{1,0:T(8,128)(2,1)}, f32[2,10,384]{2,1,0:T(8,128)}) custom-call(s32[3]{0:T(128)} %pad_add_fusion.fsel_ref, s32[2]{0:T(128)} %pad_add_fusion.6.rs_ref, bf16[384,1280]{1,0:T(8,128)(2,1)} %copy-done.14, bf16[3,128,1280]{2,1,0:T(8,128)(2,1)} %get-tuple-element.176.kf0_ref.kf1_ref, ...), custom_call_target="tpu_custom_call" | custom-call | tf_op jit(solution)/shard_map/pallas_call | solution.py:78
  120.4 9.4 %shard_map.110 = (bf16[1280,384]{1,0:T(8,128)(2,1)}, f32[2,10,384]{2,1,0:T(8,128)}) custom-call(s32[3]{0:T(128)} %pad_add_fusion.fsel_ref, s32[2]{0:T(128)} %pad_add_fusion.2.rs_ref, bf16[384,1280]{1,0:T(8,128)(2,1)} %copy-done.9, bf16[3,128,1280]{2,1,0:T(8,128)(2,1)} %get-tuple-element.177.kf0_ref.kf1_ref, ...), custom_call_target="tpu_custom_call" | custom-call | tf_op jit(solution)/shard_map/pallas_call | solution.py:78
  130.7 2.9 fusion.26
  138.8 9.4 %shard_map.119 = (bf16[1280,384]{1,0:T(8,128)(2,1)}, f32[2,10,384]{2,1,0:T(8,128)}) custom-call(s32[3]{0:T(128)} %pad_add_fusion.fsel_ref, s32[2]{0:T(128)} %pad_add_fusion.5.rs_ref, bf16[384,1280]{1,0:T(8,128)(2,1)} %copy-done.13, bf16[3,128,1280]{2,1,0:T(8,128)(2,1)} %get-tuple-element.176.kf0_ref.kf1_ref, ...), custom_call_target="tpu_custom_call" | custom-call | tf_op jit(solution)/shard_map/pallas_call | solution.py:78
  148.2 8.5 %collective-permute-done.26 = f32[2,10,384]{2,1,0:T(8,128)S(1)} collective-permute-done((f32[2,10,384]{2,1,0:T(8,128)S(1)}, f32[2,10,384]{2,1,0:T(8,128)S(1)}, u32[]{:S(2)}, u32[]{:S(2)}) %collective-permute-start.26) | collective-permute-done | bytes 30752 | tf_op jit(solution)/shard_map/ppermute | solution.py:175
  159.0 2.8 fusion.11
  164.4 9.4 %shard_map.111 = (bf16[1280,384]{1,0:T(8,128)(2,1)}, f32[2,10,384]{2,1,0:T(8,128)}) custom-call(s32[3]{0:T(128)} %pad_add_fusion.fsel_ref, s32[2]{0:T(128)} %pad_add_fusion.3.rs_ref, bf16[384,1280]{1,0:T(8,128)(2,1)} %copy-done.8, bf16[3,128,1280]{2,1,0:T(8,128)(2,1)} %get-tuple-element.177.kf0_ref.kf1_ref, ...), custom_call_target="tpu_custom_call" | custom-call | tf_op jit(solution)/shard_map/pallas_call | solution.py:78
  174.6 2.9 fusion.24
  182.7 9.4 %shard_map.120 = (bf16[1280,384]{1,0:T(8,128)(2,1)}, f32[2,10,384]{2,1,0:T(8,128)}) custom-call(s32[3]{0:T(128)} %pad_add_fusion.fsel_ref, s32[2]{0:T(128)} %pad_add_fusion.4.rs_ref, bf16[384,1280]{1,0:T(8,128)(2,1)} %copy-done.12, bf16[3,128,1280]{2,1,0:T(8,128)(2,1)} %get-tuple-element.176.kf0_ref.kf1_ref, ...), custom_call_target="tpu_custom_call" | custom-call | tf_op jit(solution)/shard_map/pallas_call | solution.py:78
  192.1 8.4 %collective-permute-done.29 = f32[2,10,384]{2,1,0:T(8,128)S(1)} collective-permute-done((f32[2,10,384]{2,1,0:T(8,128)S(1)}, f32[2,10,384]{2,1,0:T(8,128)S(1)}, u32[]{:S(2)}, u32[]{:S(2)}) %collective-permute-start.29) | collective-permute-done | bytes 30752 | tf_op jit(solution)/shard_map/ppermute | solution.py:175
  202.9 2.8 fusion.9
  208.3 9.4 %shard_map.112 = (bf16[1280,384]{1,0:T(8,128)(2,1)}, f32[2,10,384]{2,1,0:T(8,128)}) custom-call(s32[3]{0:T(128)} %pad_add_fusion.fsel_ref, s32[2]{0:T(128)} %pad_add_fusion.4.rs_ref, bf16[384,1280]{1,0:T(8,128)(2,1)} %copy-done.7, bf16[3,128,1280]{2,1,0:T(8,128)(2,1)} %get-tuple-element.177.kf0_ref.kf1_ref, ...), custom_call_target="tpu_custom_call" | custom-call | tf_op jit(solution)/shard_map/pallas_call | solution.py:78
  218.6 2.9 fusion.22
  226.6 9.4 %shard_map.121 = (bf16[1280,384]{1,0:T(8,128)(2,1)}, f32[2,10,384]{2,1,0:T(8,128)}) custom-call(s32[3]{0:T(128)} %pad_add_fusion.fsel_ref, s32[2]{0:T(128)} %pad_add_fusion.3.rs_ref, bf16[384,1280]{1,0:T(8,128)(2,1)} %copy-done.10, bf16[3,128,1280]{2,1,0:T(8,128)(2,1)} %get-tuple-element.176.kf0_ref.kf1_ref, ...), custom_call_target="tpu_custom_call" | custom-call | tf_op jit(solution)/shard_map/pallas_call | solution.py:78
  236.0 8.4 %collective-permute-done.32 = f32[2,10,384]{2,1,0:T(8,128)S(1)} collective-permute-done((f32[2,10,384]{2,1,0:T(8,128)S(1)}, f32[2,10,384]{2,1,0:T(8,128)S(1)}, u32[]{:S(2)}, u32[]{:S(2)}) %collective-permute-start.32) | collective-permute-done | bytes 30752 | tf_op jit(solution)/shard_map/ppermute | solution.py:175
  252.2 9.4 %shard_map.113 = (bf16[1280,384]{1,0:T(8,128)(2,1)}, f32[2,10,384]{2,1,0:T(8,128)}) custom-call(s32[3]{0:T(128)} %pad_add_fusion.fsel_ref, s32[2]{0:T(128)} %pad_add_fusion.5.rs_ref, bf16[384,1280]{1,0:T(8,128)(2,1)} %copy-done.6, bf16[3,128,1280]{2,1,0:T(8,128)(2,1)} %get-tuple-element.177.kf0_ref.kf1_ref, ...), custom_call_target="tpu_custom_call" | custom-call | tf_op jit(solution)/shard_map/pallas_call | solution.py:78
  270.6 9.4 %shard_map.122 = (bf16[1280,384]{1,0:T(8,128)(2,1)}, f32[2,10,384]{2,1,0:T(8,128)}) custom-call(s32[3]{0:T(128)} %pad_add_fusion.fsel_ref, s32[2]{0:T(128)} %pad_add_fusion.2.rs_ref, bf16[384,1280]{1,0:T(8,128)(2,1)} %copy-done.11, bf16[3,128,1280]{2,1,0:T(8,128)(2,1)} %get-tuple-element.176.kf0_ref.kf1_ref, ...), custom_call_target="tpu_custom_call" | custom-call | tf_op jit(solution)/shard_map/pallas_call | solution.py:78
  280.0 8.4 %collective-permute-done.35 = f32[2,10,384]{2,1,0:T(8,128)S(1)} collective-permute-done((f32[2,10,384]{2,1,0:T(8,128)S(1)}, f32[2,10,384]{2,1,0:T(8,128)S(1)}, u32[]{:S(2)}, u32[]{:S(2)}) %collective-permute-start.35) | collective-permute-done | bytes 30752 | tf_op jit(solution)/shard_map/ppermute | solution.py:175
  290.8 2.9 fusion.5
  296.2 9.4 %shard_map.114 = (bf16[1280,384]{1,0:T(8,128)(2,1)}, f32[2,10,384]{2,1,0:T(8,128)}) custom-call(s32[3]{0:T(128)} %pad_add_fusion.fsel_ref, s32[2]{0:T(128)} %pad_add_fusion.6.rs_ref, bf16[384,1280]{1,0:T(8,128)(2,1)} %copy-done.5, bf16[3,128,1280]{2,1,0:T(8,128)(2,1)} %get-tuple-element.177.kf0_ref.kf1_ref, ...), custom_call_target="tpu_custom_call" | custom-call | tf_op jit(solution)/shard_map/pallas_call | solution.py:78
  314.5 9.4 %shard_map.123 = (bf16[1280,384]{1,0:T(8,128)(2,1)}, f32[2,10,384]{2,1,0:T(8,128)}) custom-call(s32[3]{0:T(128)} %pad_add_fusion.fsel_ref, s32[2]{0:T(128)} %pad_add_fusion.1.rs_ref, bf16[384,1280]{1,0:T(8,128)(2,1)} %copy-done.16, bf16[3,128,1280]{2,1,0:T(8,128)(2,1)} %get-tuple-element.176.kf0_ref.kf1_ref, ...), custom_call_target="tpu_custom_call" | custom-call | tf_op jit(solution)/shard_map/pallas_call | solution.py:78
  323.9 5.9 %collective-permute-done.38 = f32[2,10,384]{2,1,0:T(8,128)S(1)} collective-permute-done((f32[2,10,384]{2,1,0:T(8,128)S(1)}, f32[2,10,384]{2,1,0:T(8,128)S(1)}, u32[]{:S(2)}, u32[]{:S(2)}) %collective-permute-start.38) | collective-permute-done | bytes 30752 | tf_op jit(solution)/shard_map/ppermute | solution.py:175
  335.1 9.5 %shard_map.115 = (bf16[1280,384]{1,0:T(8,128)(2,1)}, f32[2,10,384]{2,1,0:T(8,128)}) custom-call(s32[3]{0:T(128)} %pad_add_fusion.fsel_ref, s32[2]{0:T(128)} %pad_add_fusion.7.rs_ref, bf16[384,1280]{1,0:T(8,128)(2,1)} %copy-done.15, bf16[3,128,1280]{2,1,0:T(8,128)(2,1)} %get-tuple-element.177.kf0_ref.kf1_ref, ...), custom_call_target="tpu_custom_call" | custom-call | tf_op jit(solution)/shard_map/pallas_call | solution.py:78
  352.1 13.3 %collective-permute-done.20 = f32[2,10,384]{2,1,0:T(8,128)S(1)} collective-permute-done((f32[2,10,384]{2,1,0:T(8,128)S(1)}, f32[2,10,384]{2,1,0:T(8,128)S(1)}, u32[]{:S(2)}, u32[]{:S(2)}) %collective-permute-start.20) | collective-permute-done | bytes 30752 | tf_op jit(solution)/shard_map/ppermute | solution.py:182
  367.8 16.8 %convolution_convert_fusion = bf16[384,5120]{1,0:T(8,128)(2,1)} fusion(bf16[2560,384]{1,0:T(8,128)(2,1)S(1)} %fusion, bf16[2560,5120]{1,0:T(8,128)(2,1)} %param.19), kind=kOutput, calls=%fused_computation.1 | convolution fusion | flops 10068295680 | bytes 32112640 | tf_op jit(solution)/shard_map/dot_general | solution.py:188
  384.7 51.5 %reduce-scatter.2.cloned.1.call-done = bf16[192,5120]{1,0:T(8,128)(2,1)} async-done(((bf16[384,5120]{1,0:T(8,128)(2,1)}), bf16[192,5120]{1,0:T(8,128)(2,1)}) %reduce-scatter.2.cloned.1.call-update) | async-done | bytes 1966096 | tf_op jit(solution)/shard_map/reduce_scatter | solution.py:191
  (231 shorter events, 113.1 us)
Async XLA Ops:
  6.5 429.7 %reduce-scatter.2.cloned.1.call-start = ((), (), s32[]{:S(2)}) async-start(), calls=%async_computation.1 | async-start | bytes 5898240 | tf_op jit(solution)/shard_map/reduce_scatter | solution.py:191
  8.3 34.3 %collective-permute-start.21 = (bf16[384,1280]{1,0:T(8,128)(2,1)S(1)}, bf16[384,1280]{1,0:T(8,128)(2,1)}, u32[]{:S(2)}, u32[]{:S(2)}) collective-permute-start(bf16[384,1280]{1,0:T(8,128)(2,1)S(1)} %get-tuple-element.118.q_ref), channel_id=1, source_target_pairs={{0,4},{8,0},{16,8},{24,16},{28,24},{20,28},{12,20},{4,12},{1,5},{9... | collective-permute-start | bytes 2949128 | tf_op jit(solution)/shard_map/ppermute | solution.py:174
  11.3 47.1 %collective-permute-start = (bf16[384,1280]{1,0:T(8,128)(2,1)S(1)}, bf16[384,1280]{1,0:T(8,128)(2,1)S(1)}, u32[]{:S(2)}, u32[]{:S(2)}) collective-permute-start(bf16[384,1280]{1,0:T(8,128)(2,1)S(1)} %get-tuple-element.117.q_ref), channel_id=1, source_target_pairs={{0,8},{8,16},{16,24},{24,28},{28,20},{20,12},{12,4},{4,0},{1,9},{9... | collective-permute-start | bytes 2949128 | tf_op jit(solution)/shard_map/ppermute | solution.py:174
  42.6 59.8 %collective-permute-start.24 = (bf16[384,1280]{1,0:T(8,128)(2,1)}, bf16[384,1280]{1,0:T(8,128)(2,1)S(1)}, u32[]{:S(2)}, u32[]{:S(2)}) collective-permute-start(bf16[384,1280]{1,0:T(8,128)(2,1)} %collective-permute-done.21.q_ref), channel_id=1, source_target_pairs={{0,4},{8,0},{16,8},{24,16},{28,24},{20,28},{12,20},{4,12},{1,5},{9... | collective-permute-start | bytes 2949128 | tf_op jit(solution)/shard_map/ppermute | solution.py:174
  56.8 58.2 %collective-permute-start.22 = (bf16[1280,384]{1,0:T(8,128)(2,1)}, bf16[1280,384]{1,0:T(8,128)(2,1)}, u32[]{:S(2)}, u32[]{:S(2)}) collective-permute-start(bf16[1280,384]{1,0:T(8,128)(2,1)} %get-tuple-element.59), channel_id=1, source_target_pairs={{0,4},{8,0},{16,8},{24,16},{28,24},{20,28},{12,20},{4,12},{1,5},{9... | collective-permute-start | bytes 2949128 | tf_op jit(solution)/shard_map/ppermute | solution.py:175
  58.4 61.1 %collective-permute-start.3 = (bf16[384,1280]{1,0:T(8,128)(2,1)S(1)}, bf16[384,1280]{1,0:T(8,128)(2,1)S(1)}, u32[]{:S(2)}, u32[]{:S(2)}) collective-permute-start(bf16[384,1280]{1,0:T(8,128)(2,1)S(1)} %collective-permute-done.q_ref), channel_id=1, source_target_pairs={{0,8},{8,16},{16,24},{24,28},{28,20},{20,12},{12,4},{4,0},{1,9},{9... | collective-permute-start | bytes 2949128 | tf_op jit(solution)/shard_map/ppermute | solution.py:174
  72.2 58.4 %collective-permute-start.1 = (bf16[1280,384]{1,0:T(8,128)(2,1)}, bf16[1280,384]{1,0:T(8,128)(2,1)}, u32[]{:S(2)}, u32[]{:S(2)}) collective-permute-start(bf16[1280,384]{1,0:T(8,128)(2,1)} %get-tuple-element.43), channel_id=1, source_target_pairs={{0,8},{8,16},{16,24},{24,28},{28,20},{20,12},{12,4},{4,0},{1,9},{9... | collective-permute-start | bytes 2949128 | tf_op jit(solution)/shard_map/ppermute | solution.py:175
  79.7 33.0 %collective-permute-start.23 = (f32[2,10,384]{2,1,0:T(8,128)S(1)}, f32[2,10,384]{2,1,0:T(8,128)S(1)}, u32[]{:S(2)}, u32[]{:S(2)}) collective-permute-start(f32[2,10,384]{2,1,0:T(8,128)S(1)} %copy-done.38), channel_id=1, source_target_pairs={{0,4},{8,0},{16,8},{24,16},{28,24},{20,28},{12,20},{4,12},{1,5},{9... | collective-permute-start | bytes 92168 | tf_op jit(solution)/shard_map/ppermute | solution.py:175
  102.3 27.5 %collective-permute-start.2 = (f32[2,10,384]{2,1,0:T(8,128)S(1)}, f32[2,10,384]{2,1,0:T(8,128)S(1)}, u32[]{:S(2)}, u32[]{:S(2)}) collective-permute-start(f32[2,10,384]{2,1,0:T(8,128)S(1)} %copy-done.37), channel_id=1, source_target_pairs={{0,8},{8,16},{16,24},{24,28},{28,20},{20,12},{12,4},{4,0},{1,9},{9... | collective-permute-start | bytes 92168 | tf_op jit(solution)/shard_map/ppermute | solution.py:175
  112.7 24.8 %collective-permute-start.27 = (bf16[384,1280]{1,0:T(8,128)(2,1)}, bf16[384,1280]{1,0:T(8,128)(2,1)S(1)}, u32[]{:S(2)}, u32[]{:S(2)}) collective-permute-start(bf16[384,1280]{1,0:T(8,128)(2,1)} %copy-done.14), channel_id=1, source_target_pairs={{0,4},{8,0},{16,8},{24,16},{28,24},{20,28},{12,20},{4,12},{1,5},{9... | collective-permute-start | bytes 2949128 | tf_op jit(solution)/shard_map/ppermute | solution.py:174
  117.9 41.1 %collective-permute-start.25 = (bf16[1280,384]{1,0:T(8,128)(2,1)}, bf16[1280,384]{1,0:T(8,128)(2,1)}, u32[]{:S(2)}, u32[]{:S(2)}) collective-permute-start(bf16[1280,384]{1,0:T(8,128)(2,1)} %fusion.13), channel_id=1, source_target_pairs={{0,4},{8,0},{16,8},{24,16},{28,24},{20,28},{12,20},{4,12},{1,5},{9... | collective-permute-start | bytes 2949128 | tf_op jit(solution)/shard_map/ppermute | solution.py:175
  119.5 43.9 %collective-permute-start.6 = (bf16[384,1280]{1,0:T(8,128)(2,1)S(1)}, bf16[384,1280]{1,0:T(8,128)(2,1)S(1)}, u32[]{:S(2)}, u32[]{:S(2)}) collective-permute-start(bf16[384,1280]{1,0:T(8,128)(2,1)S(1)} %collective-permute-done.3.q_ref), channel_id=1, source_target_pairs={{0,8},{8,16},{16,24},{24,28},{28,20},{20,12},{12,4},{4,0},{1,9},{9... | collective-permute-start | bytes 2949128 | tf_op jit(solution)/shard_map/ppermute | solution.py:174
  133.5 41.1 %collective-permute-start.4 = (bf16[1280,384]{1,0:T(8,128)(2,1)}, bf16[1280,384]{1,0:T(8,128)(2,1)}, u32[]{:S(2)}, u32[]{:S(2)}) collective-permute-start(bf16[1280,384]{1,0:T(8,128)(2,1)} %fusion.26), channel_id=1, source_target_pairs={{0,8},{8,16},{16,24},{24,28},{28,20},{20,12},{12,4},{4,0},{1,9},{9... | collective-permute-start | bytes 2949128 | tf_op jit(solution)/shard_map/ppermute | solution.py:175
  137.5 36.3 %collective-permute-start.5 = (f32[2,10,384]{2,1,0:T(8,128)S(1)}, f32[2,10,384]{2,1,0:T(8,128)S(1)}, u32[]{:S(2)}, u32[]{:S(2)}) collective-permute-start(f32[2,10,384]{2,1,0:T(8,128)S(1)} %pad_maximum_fusion), channel_id=1, source_target_pairs={{0,8},{8,16},{16,24},{24,28},{28,20},{20,12},{12,4},{4,0},{1,9},{9... | collective-permute-start | bytes 92168 | tf_op jit(solution)/shard_map/ppermute | solution.py:175
  161.8 41.1 %collective-permute-start.28 = (bf16[1280,384]{1,0:T(8,128)(2,1)}, bf16[1280,384]{1,0:T(8,128)(2,1)}, u32[]{:S(2)}, u32[]{:S(2)}) collective-permute-start(bf16[1280,384]{1,0:T(8,128)(2,1)} %fusion.11), channel_id=1, source_target_pairs={{0,4},{8,0},{16,8},{24,16},{28,24},{20,28},{12,20},{4,12},{1,5},{9... | collective-permute-start | bytes 2949128 | tf_op jit(solution)/shard_map/ppermute | solution.py:175
  163.4 43.9 %collective-permute-start.9 = (bf16[384,1280]{1,0:T(8,128)(2,1)S(1)}, bf16[384,1280]{1,0:T(8,128)(2,1)S(1)}, u32[]{:S(2)}, u32[]{:S(2)}) collective-permute-start(bf16[384,1280]{1,0:T(8,128)(2,1)S(1)} %collective-permute-done.6.q_ref), channel_id=1, source_target_pairs={{0,8},{8,16},{16,24},{24,28},{28,20},{20,12},{12,4},{4,0},{1,9},{9... | collective-permute-start | bytes 2949128 | tf_op jit(solution)/shard_map/ppermute | solution.py:174
  177.5 41.1 %collective-permute-start.7 = (bf16[1280,384]{1,0:T(8,128)(2,1)}, bf16[1280,384]{1,0:T(8,128)(2,1)}, u32[]{:S(2)}, u32[]{:S(2)}) collective-permute-start(bf16[1280,384]{1,0:T(8,128)(2,1)} %fusion.24), channel_id=1, source_target_pairs={{0,8},{8,16},{16,24},{24,28},{28,20},{20,12},{12,4},{4,0},{1,9},{9... | collective-permute-start | bytes 2949128 | tf_op jit(solution)/shard_map/ppermute | solution.py:175
  181.5 36.3 %collective-permute-start.8 = (f32[2,10,384]{2,1,0:T(8,128)S(1)}, f32[2,10,384]{2,1,0:T(8,128)S(1)}, u32[]{:S(2)}, u32[]{:S(2)}) collective-permute-start(f32[2,10,384]{2,1,0:T(8,128)S(1)} %pad_maximum_fusion.1), channel_id=1, source_target_pairs={{0,8},{8,16},{16,24},{24,28},{28,20},{20,12},{12,4},{4,0},{1,9},{9... | collective-permute-start | bytes 92168 | tf_op jit(solution)/shard_map/ppermute | solution.py:175
  205.8 41.1 %collective-permute-start.31 = (bf16[1280,384]{1,0:T(8,128)(2,1)}, bf16[1280,384]{1,0:T(8,128)(2,1)}, u32[]{:S(2)}, u32[]{:S(2)}) collective-permute-start(bf16[1280,384]{1,0:T(8,128)(2,1)} %fusion.9), channel_id=1, source_target_pairs={{0,4},{8,0},{16,8},{24,16},{28,24},{20,28},{12,20},{4,12},{1,5},{9... | collective-permute-start | bytes 2949128 | tf_op jit(solution)/shard_map/ppermute | solution.py:175
  207.3 43.9 %collective-permute-start.12 = (bf16[384,1280]{1,0:T(8,128)(2,1)S(1)}, bf16[384,1280]{1,0:T(8,128)(2,1)S(1)}, u32[]{:S(2)}, u32[]{:S(2)}) collective-permute-start(bf16[384,1280]{1,0:T(8,128)(2,1)S(1)} %collective-permute-done.9.q_ref), channel_id=1, source_target_pairs={{0,8},{8,16},{16,24},{24,28},{28,20},{20,12},{12,4},{4,0},{1,9},{9... | collective-permute-start | bytes 2949128 | tf_op jit(solution)/shard_map/ppermute | solution.py:174
  221.5 41.0 %collective-permute-start.10 = (bf16[1280,384]{1,0:T(8,128)(2,1)}, bf16[1280,384]{1,0:T(8,128)(2,1)}, u32[]{:S(2)}, u32[]{:S(2)}) collective-permute-start(bf16[1280,384]{1,0:T(8,128)(2,1)} %fusion.22), channel_id=1, source_target_pairs={{0,8},{8,16},{16,24},{24,28},{28,20},{20,12},{12,4},{4,0},{1,9},{9... | collective-permute-start | bytes 2949128 | tf_op jit(solution)/shard_map/ppermute | solution.py:175
  225.4 36.3 %collective-permute-start.11 = (f32[2,10,384]{2,1,0:T(8,128)S(1)}, f32[2,10,384]{2,1,0:T(8,128)S(1)}, u32[]{:S(2)}, u32[]{:S(2)}) collective-permute-start(f32[2,10,384]{2,1,0:T(8,128)S(1)} %pad_maximum_fusion.2), channel_id=1, source_target_pairs={{0,8},{8,16},{16,24},{24,28},{28,20},{20,12},{12,4},{4,0},{1,9},{9... | collective-permute-start | bytes 92168 | tf_op jit(solution)/shard_map/ppermute | solution.py:175
  249.7 41.1 %collective-permute-start.34 = (bf16[1280,384]{1,0:T(8,128)(2,1)}, bf16[1280,384]{1,0:T(8,128)(2,1)}, u32[]{:S(2)}, u32[]{:S(2)}) collective-permute-start(bf16[1280,384]{1,0:T(8,128)(2,1)} %fusion.7), channel_id=1, source_target_pairs={{0,4},{8,0},{16,8},{24,16},{28,24},{20,28},{12,20},{4,12},{1,5},{9... | collective-permute-start | bytes 2949128 | tf_op jit(solution)/shard_map/ppermute | solution.py:175
  251.3 44.0 %collective-permute-start.15 = (bf16[384,1280]{1,0:T(8,128)(2,1)S(1)}, bf16[384,1280]{1,0:T(8,128)(2,1)S(1)}, u32[]{:S(2)}, u32[]{:S(2)}) collective-permute-start(bf16[384,1280]{1,0:T(8,128)(2,1)S(1)} %collective-permute-done.12.q_ref), channel_id=1, source_target_pairs={{0,8},{8,16},{16,24},{24,28},{28,20},{20,12},{12,4},{4,0},{1,9},{9... | collective-permute-start | bytes 2949128 | tf_op jit(solution)/shard_map/ppermute | solution.py:174
  265.3 41.1 %collective-permute-start.13 = (bf16[1280,384]{1,0:T(8,128)(2,1)}, bf16[1280,384]{1,0:T(8,128)(2,1)}, u32[]{:S(2)}, u32[]{:S(2)}) collective-permute-start(bf16[1280,384]{1,0:T(8,128)(2,1)} %fusion.20), channel_id=1, source_target_pairs={{0,8},{8,16},{16,24},{24,28},{28,20},{20,12},{12,4},{4,0},{1,9},{9... | collective-permute-start | bytes 2949128 | tf_op jit(solution)/shard_map/ppermute | solution.py:175
  269.3 36.3 %collective-permute-start.14 = (f32[2,10,384]{2,1,0:T(8,128)S(1)}, f32[2,10,384]{2,1,0:T(8,128)S(1)}, u32[]{:S(2)}, u32[]{:S(2)}) collective-permute-start(f32[2,10,384]{2,1,0:T(8,128)S(1)} %pad_maximum_fusion.3), channel_id=1, source_target_pairs={{0,8},{8,16},{16,24},{24,28},{28,20},{20,12},{12,4},{4,0},{1,9},{9... | collective-permute-start | bytes 92168 | tf_op jit(solution)/shard_map/ppermute | solution.py:175
  288.4 24.8 %collective-permute-start.39 = (bf16[384,1280]{1,0:T(8,128)(2,1)}, bf16[384,1280]{1,0:T(8,128)(2,1)S(1)}, u32[]{:S(2)}, u32[]{:S(2)}) collective-permute-start(bf16[384,1280]{1,0:T(8,128)(2,1)} %copy-done.11), channel_id=1, source_target_pairs={{0,4},{8,0},{16,8},{24,16},{28,24},{20,28},{12,20},{4,12},{1,5},{9... | collective-permute-start | bytes 2949128 | tf_op jit(solution)/shard_map/ppermute | solution.py:174
  293.6 37.0 %collective-permute-start.37 = (bf16[1280,384]{1,0:T(8,128)(2,1)}, bf16[1280,384]{1,0:T(8,128)(2,1)}, u32[]{:S(2)}, u32[]{:S(2)}) collective-permute-start(bf16[1280,384]{1,0:T(8,128)(2,1)} %fusion.5), channel_id=1, source_target_pairs={{0,4},{8,0},{16,8},{24,16},{28,24},{20,28},{12,20},{4,12},{1,5},{9... | collective-permute-start | bytes 2949128 | tf_op jit(solution)/shard_map/ppermute | solution.py:175
  295.2 38.9 %collective-permute-start.18 = (bf16[384,1280]{1,0:T(8,128)(2,1)S(1)}, bf16[384,1280]{1,0:T(8,128)(2,1)S(1)}, u32[]{:S(2)}, u32[]{:S(2)}) collective-permute-start(bf16[384,1280]{1,0:T(8,128)(2,1)S(1)} %collective-permute-done.15.q_ref), channel_id=1, source_target_pairs={{0,8},{8,16},{16,24},{24,28},{28,20},{20,12},{12,4},{4,0},{1,9},{9... | collective-permute-start | bytes 2949128 | tf_op jit(solution)/shard_map/ppermute | solution.py:174
  309.3 36.1 %collective-permute-start.16 = (bf16[1280,384]{1,0:T(8,128)(2,1)}, bf16[1280,384]{1,0:T(8,128)(2,1)}, u32[]{:S(2)}, u32[]{:S(2)}) collective-permute-start(bf16[1280,384]{1,0:T(8,128)(2,1)} %fusion.18), channel_id=1, source_target_pairs={{0,8},{8,16},{16,24},{24,28},{28,20},{20,12},{12,4},{4,0},{1,9},{9... | collective-permute-start | bytes 2949128 | tf_op jit(solution)/shard_map/ppermute | solution.py:175
  313.3 31.3 %collective-permute-start.17 = (f32[2,10,384]{2,1,0:T(8,128)S(1)}, f32[2,10,384]{2,1,0:T(8,128)S(1)}, u32[]{:S(2)}, u32[]{:S(2)}) collective-permute-start(f32[2,10,384]{2,1,0:T(8,128)S(1)} %pad_maximum_fusion.4), channel_id=1, source_target_pairs={{0,8},{8,16},{16,24},{24,28},{28,20},{20,12},{12,4},{4,0},{1,9},{9... | collective-permute-start | bytes 92168 | tf_op jit(solution)/shard_map/ppermute | solution.py:175
  332.5 33.0 %collective-permute-start.40 = (bf16[1280,384]{1,0:T(8,128)(2,1)S(1)}, bf16[1280,384]{1,0:T(8,128)(2,1)}, u32[]{:S(2)}, u32[]{:S(2)}) collective-permute-start(bf16[1280,384]{1,0:T(8,128)(2,1)S(1)} %fusion.3), channel_id=1, source_target_pairs={{0,4},{8,0},{16,8},{24,16},{28,24},{20,28},{12,20},{4,12},{1,5},{9... | collective-permute-start | bytes 2949128 | tf_op jit(solution)/shard_map/ppermute | solution.py:182
  (51 other events, 529.6 us)
Sparse Core Ops, SparseCore 0:
  384.8 51.3 reduce-scatter.1
where the time goes:
time: 446 us; the launch traced here: 443 us
  Pallas kernels  151 us (34%)
  waiting for transfers between devices  115 us (26%)
  other arithmetic  63.2 us (14%)
  starting transfers between devices  48.8 us (11%)
  between operations  33.1 us (7%)
  matrix products  16.8 us (4%)
  local copies, waits for them, and re-layouts  14.9 us (3%)
    pallas_call x16, Pallas kernels, attend_part(): pl.pallas_call(part_kernel, grid_spec=pltpu.PrefetchScalarGridSpec(num_sc...  151 us
    reduce_scatter x1, waiting for transfers between devices, on_device(): lax.psum_scatter(mixed.astype(jnp.bfloat16), 'head', scatter_dimension=0,...  51.5 us
    ppermute x24, waiting for transfers between devices, on_device(): lax.ppermute(run[h], 'seq', perms[h])  39.7 us
    convert_element_type x12, other arithmetic, on_device(): run[h] = (run[h][0].astype(jnp.bfloat16), run[h][1])  32.3 us
    ppermute x24, starting transfers between devices, on_device(): lax.ppermute(run[h], 'seq', perms[h])  28.5 us
    dot_general x1, matrix products, on_device(): lax.dot_general(attended, out_weight, (((0,), (0,)), ((), ())), preferred...  16.8 us
    ppermute x14, starting transfers between devices, on_device(): got_q = [lax.ppermute(moving[h], 'seq', perms[h]) for h in range(2)]  15.8 us
    ppermute x4, waiting for transfers between devices, on_device(): got_run = [lax.ppermute(run[h], 'seq', perms[h]) for h in range(2)]  15.1 us
  transfers between devices with their start and end apart: 43, of which 13 were waited for; matrix products, arithmetic and copies ran while one was open for 16% of the time, Pallas kernels for 34%

commit v1 on v0

--- a/solution.py
+++ b/solution.py
@@ -167,28 +167,52 @@
         rs = jnp.stack([sidx[reader], sval[reader]])
         return attend_part(q, fsel, rs, k3, v3, s3, t3)
 
-    moving = [halves[0][0], halves[1][0]]
-    run = [None, None]
     perms = (forward, backward)
-    for t in range(1, readers):
-        got_q = [lax.ppermute(moving[h], "seq", perms[h]) for h in range(2)]
-        got_run = [None, None] if t == 1 else [lax.ppermute(run[h], "seq", perms[h]) for h in range(2)]
-        readers_t = (ring_arr[(pos - t + readers) % readers], ring_arr[(pos + t) % readers])
-        for h in range(2):
-            mine = own(h, got_q[h], readers_t[h])
-            run[h] = mine if t == 1 else combine(got_run[h], mine)
-            run[h] = (run[h][0].astype(jnp.bfloat16), run[h][1])
-        moving = got_q
-    got_run = [lax.ppermute(run[h], "seq", perms[h]) for h in range(2)]
-    run_f = combine(got_run[0], own(0, halves[0][0], me))
-    run_b = combine(got_run[1], own(1, halves[1][0], me))
-    acc = jnp.concatenate([run_f[0], run_b[0]], axis=0)
-    total = jnp.concatenate([run_f[1][1], run_b[1][1]], axis=0)
-    attended = (acc / jnp.repeat(total, HD, axis=0)).astype(jnp.bfloat16)
-    mixed = lax.dot_general(
-        attended, out_weight, (((0,), (0,)), ((), ())), preferred_element_type=jnp.float32
+
+    def run_ring(q_part):
+        mine = [q_part[:, :cut], q_part[:, cut:]]
+        moving = list(mine)
+        run = [None, None]
+        for t in range(1, readers):
+            got_q = [lax.ppermute(moving[h], "seq", perms[h]) for h in range(2)]
+            got_run = [None, None] if t == 1 else [lax.ppermute(run[h], "seq", perms[h]) for h in range(2)]
+            readers_t = (ring_arr[(pos - t + readers) % readers], ring_arr[(pos + t) % readers])
+            for h in range(2):
+                part = own(h, got_q[h], readers_t[h])
+                run[h] = part if t == 1 else combine(got_run[h], part)
+                run[h] = (run[h][0].astype(jnp.bfloat16), run[h][1])
+            moving = got_q
+        got_run = [lax.ppermute(run[h], "seq", perms[h]) for h in range(2)]
+        fin = [combine(got_run[h], own(h, mine[h], me)) for h in range(2)]
+        acc = jnp.concatenate([fin[0][0], fin[1][0]], axis=0)
+        total = jnp.concatenate([fin[0][1][1], fin[1][1][1]], axis=0)
+        return (acc / jnp.repeat(total, HD, axis=0)).astype(jnp.bfloat16)
+
+    contract = (((0,), (0,)), ((), ()))
+    n_head = out_weight.shape[1] // width_here
+    rows = tokens_here // 2
+    big = tokens_here - TILE
+    if n_head != 2 or big < rows:
+        attended = run_ring(queries)
+        mixed = lax.dot_general(attended, out_weight, contract, preferred_element_type=jnp.float32)
+        return lax.psum_scatter(mixed.astype(jnp.bfloat16), "head", scatter_dimension=0, tiled=True)
+    hid = lax.axis_index("head")
+    start1 = (1 - hid) * TILE
+    start2 = hid * big
+    first = run_ring(lax.dynamic_slice_in_dim(queries, start1, big, 0))
+    theirs = lax.dynamic_slice_in_dim(first, (1 - hid) * (big - rows), rows, 1)
+    sent = lax.dot_general(theirs, out_weight, contract, preferred_element_type=jnp.float32)
+    got = lax.ppermute(sent.astype(jnp.bfloat16), "head", [(0, 1), (1, 0)])
+    first, rest_q = lax.optimization_barrier(
+        (first, lax.dynamic_slice_in_dim(queries, start2, TILE, 0))
     )
-    return lax.psum_scatter(mixed.astype(jnp.bfloat16), "head", scatter_dimension=0, tiled=True)
+    second = run_ring(rest_q)
+    full = jnp.zeros((width_here, tokens_here), jnp.bfloat16)
+    full = lax.dynamic_update_slice_in_dim(full, first, start1, 1)
+    full = lax.dynamic_update_slice_in_dim(full, second, start2, 1)
+    ours = lax.dynamic_slice_in_dim(full, hid * rows, rows, 1)
+    kept = lax.dot_general(ours, out_weight, contract, preferred_element_type=jnp.float32)
+    return (kept.astype(jnp.bfloat16).astype(jnp.float32) + got.astype(jnp.float32)).astype(jnp.bfloat16)
 
 
 def solution(mesh):

time: 446 us -> 591 us (1.33)
  Pallas kernels: 151 us -> 253 us
  starting transfers between devices: 48.8 us -> 90.8 us
  other arithmetic: 63.2 us -> 81.7 us
  waiting for transfers between devices: 115 us -> 98 us
  between operations: 33.1 us -> 20.6 us
  matrix products: 16.8 us -> 26.4 us
    pallas_call x16 -> x32, Pallas kernels: 151 us -> 253 us  [attend_part(): pl.pallas_call(part_kernel, grid_spec=pltpu.PrefetchScalarGridSpec(num_sc...]
    reduce_scatter x1 -> x0, waiting for transfers between devices: 51.5 us -> none  [on_device(): lax.psum_scatter(mixed.astype(jnp.bfloat16), 'head', scatter_dimension=0,...]
    ppermute x42 -> x85, starting transfers between devices: 48.7 us -> 90.8 us  [the longest x48 50.9 us: run_ring(): lax.ppermute(run[h], 'seq', perms[h])]
    ppermute x42 -> x85, waiting for transfers between devices: 63.7 us -> 98 us  [the longest x28 83.4 us: run_ring(): got_q = [lax.ppermute(moving[h], 'seq', perms[h]) for h in range(2)]]
    dot_general x1 -> x2, matrix products: 16.8 us -> 26.4 us  [the longest x1 13.6 us: on_device(): lax.dot_general(ours, out_weight, contract, preferred_element_type=jnp.fl...]
    add x14 -> x28, other arithmetic: 0.27 us -> 9.01 us  [combine(): total = stat_r[1] * f_r + stat_o[1] * f_o]
    exp x12 -> x24, other arithmetic: 9.42 us -> 17.4 us  [combine(): f_r = jnp.exp(stat_r[0] - top)]
    convert_element_type x13 -> x25, other arithmetic: 32.7 us -> 33.8 us  [the longest x24 33.6 us: run_ring(): run[h] = (run[h][0].astype(jnp.bfloat16), run[h][1])]
  transfers between devices with their start and end apart: 43 -> 85, of which waited for: 13 -> 17; matrix products, arithmetic and copies ran while one was open for 16% -> 18% of each run, Pallas kernels for 34% -> 43%
where the time goes in v1:
time: 591 us; the launch traced here: 586 us
  Pallas kernels  253 us (43%)
  waiting for transfers between devices  98 us (17%)
  starting transfers between devices  90.8 us (15%)
  other arithmetic  81.7 us (14%)
  matrix products  26.4 us (4%)
  between operations  20.6 us (3%)
  local copies, waits for them, and re-layouts  15.9 us (3%)
    pallas_call x32, Pallas kernels, attend_part(): pl.pallas_call(part_kernel, grid_spec=pltpu.PrefetchScalarGridSpec(num_sc...  253 us
    ppermute x28, waiting for transfers between devices, run_ring(): got_q = [lax.ppermute(moving[h], 'seq', perms[h]) for h in range(2)]  83.4 us
    ppermute x48, starting transfers between devices, run_ring(): lax.ppermute(run[h], 'seq', perms[h])  50.9 us
    convert_element_type x24, other arithmetic, run_ring(): run[h] = (run[h][0].astype(jnp.bfloat16), run[h][1])  33.6 us
    ppermute x28, starting transfers between devices, run_ring(): got_q = [lax.ppermute(moving[h], 'seq', perms[h]) for h in range(2)]  30 us
    exp x24, other arithmetic, combine(): f_r = jnp.exp(stat_r[0] - top)  17.4 us
    another operation x8, other arithmetic, own(): rs = jnp.stack([sidx[reader], sval[reader]])  15.1 us
    ppermute x8, waiting for transfers between devices, run_ring(): got_run = [lax.ppermute(run[h], 'seq', perms[h]) for h in range(2)]  14.5 us
  transfers between devices with their start and end apart: 85, of which 17 were waited for; matrix products, arithmetic and copies ran while one was open for 18% of the time, Pallas kernels for 43%

profile of v1, /device:TPU:0, one launch (start us, length us, event | category | flops | bytes accessed | tf_op | source)
XLA Modules:
  0.0 586.0 jit_solution(13488537724345954487)
XLA Ops:
  54.2 8.6 %shard_map.117 = (bf16[1280,256]{1,0:T(8,128)(2,1)}, f32[2,10,256]{2,1,0:T(8,128)}) custom-call(s32[3]{0:T(128)} %pad_add_fusion.fsel_ref, s32[2]{0:T(128)} %pad_add_fusion.7.rs_ref, bf16[256,1280]{1,0:T(8,128)(2,1)} %collective-permute-done.21.q_ref, bf16[3,128,1280]{2,1,0:T(8,128)(2,1)} %get-tuple-element.300.kf0_ref.kf1_ref, ...), custom_call_target="tpu_custom_call" | custom-call | tf_op jit(solution)/shard_map/pallas_call | solution.py:78
  69.4 8.6 %shard_map.124 = (bf16[1280,256]{1,0:T(8,128)(2,1)}, f32[2,10,256]{2,1,0:T(8,128)}) custom-call(s32[3]{0:T(128)} %pad_add_fusion.fsel_ref, s32[2]{0:T(128)} %pad_add_fusion.8.rs_ref, bf16[256,1280]{1,0:T(8,128)(2,1)} %copy-done.1, bf16[3,128,1280]{2,1,0:T(8,128)(2,1)} %get-tuple-element.300.kf0_ref.kf1_ref, ...), custom_call_target="tpu_custom_call" | custom-call | tf_op jit(solution)/shard_map/pallas_call | solution.py:78
  78.0 8.6 %shard_map.116 = (bf16[1280,256]{1,0:T(8,128)(2,1)}, f32[2,10,256]{2,1,0:T(8,128)}) custom-call(s32[3]{0:T(128)} %pad_add_fusion.fsel_ref, s32[2]{0:T(128)} %pad_add_fusion.8.rs_ref, bf16[256,1280]{1,0:T(8,128)(2,1)} %copy-done, bf16[3,128,1280]{2,1,0:T(8,128)(2,1)} %get-tuple-element.301.kf0_ref.kf1_ref, ...), custom_call_target="tpu_custom_call" | custom-call | tf_op jit(solution)/shard_map/pallas_call | solution.py:78
  86.6 8.6 %shard_map.109 = (bf16[1280,256]{1,0:T(8,128)(2,1)}, f32[2,10,256]{2,1,0:T(8,128)}) custom-call(s32[3]{0:T(128)} %pad_add_fusion.fsel_ref, s32[2]{0:T(128)} %pad_add_fusion.1.rs_ref, bf16[256,1280]{1,0:T(8,128)(2,1)} %collective-permute-done.q_ref, bf16[3,128,1280]{2,1,0:T(8,128)(2,1)} %get-tuple-element.301.kf0_ref.kf1_ref, ...), custom_call_target="tpu_custom_call" | custom-call | tf_op jit(solution)/shard_map/pallas_call | solution.py:78
  95.8 8.6 %shard_map.118 = (bf16[1280,256]{1,0:T(8,128)(2,1)}, f32[2,10,256]{2,1,0:T(8,128)}) custom-call(s32[3]{0:T(128)} %pad_add_fusion.fsel_ref, s32[2]{0:T(128)} %pad_add_fusion.6.rs_ref, bf16[256,1280]{1,0:T(8,128)(2,1)} %collective-permute-done.24.q_ref, bf16[3,128,1280]{2,1,0:T(8,128)(2,1)} %get-tuple-element.300.kf0_ref.kf1_ref, ...), custom_call_target="tpu_custom_call" | custom-call | tf_op jit(solution)/shard_map/pallas_call | solution.py:78
  112.0 8.6 %shard_map.110 = (bf16[1280,256]{1,0:T(8,128)(2,1)}, f32[2,10,256]{2,1,0:T(8,128)}) custom-call(s32[3]{0:T(128)} %pad_add_fusion.fsel_ref, s32[2]{0:T(128)} %pad_add_fusion.2.rs_ref, bf16[256,1280]{1,0:T(8,128)(2,1)} %collective-permute-done.3.q_ref, bf16[3,128,1280]{2,1,0:T(8,128)(2,1)} %get-tuple-element.301.kf0_ref.kf1_ref, ...), custom_call_target="tpu_custom_call" | custom-call | tf_op jit(solution)/shard_map/pallas_call | solution.py:78
  123.6 12.1 %collective-permute-done.27.q_ref = bf16[256,1280]{1,0:T(8,128)(2,1)} collective-permute-done((bf16[256,1280]{1,0:T(8,128)(2,1)}, bf16[256,1280]{1,0:T(8,128)(2,1)}, u32[]{:S(2)}, u32[]{:S(2)}) %collective-permute-start.27) | collective-permute-done | bytes 655392 | tf_op jit(solution)/shard_map/ppermute | solution.py:177
  137.4 8.6 %shard_map.119 = (bf16[1280,256]{1,0:T(8,128)(2,1)}, f32[2,10,256]{2,1,0:T(8,128)}) custom-call(s32[3]{0:T(128)} %pad_add_fusion.fsel_ref, s32[2]{0:T(128)} %pad_add_fusion.5.rs_ref, bf16[256,1280]{1,0:T(8,128)(2,1)} %collective-permute-done.27.q_ref, bf16[3,128,1280]{2,1,0:T(8,128)(2,1)} %get-tuple-element.300.kf0_ref.kf1_ref, ...), custom_call_target="tpu_custom_call" | custom-call | tf_op jit(solution)/shard_map/pallas_call | solution.py:78
  152.2 8.6 %shard_map.111 = (bf16[1280,256]{1,0:T(8,128)(2,1)}, f32[2,10,256]{2,1,0:T(8,128)}) custom-call(s32[3]{0:T(128)} %pad_add_fusion.fsel_ref, s32[2]{0:T(128)} %pad_add_fusion.3.rs_ref, bf16[256,1280]{1,0:T(8,128)(2,1)} %collective-permute-done.6.q_ref, bf16[3,128,1280]{2,1,0:T(8,128)(2,1)} %get-tuple-element.301.kf0_ref.kf1_ref, ...), custom_call_target="tpu_custom_call" | custom-call | tf_op jit(solution)/shard_map/pallas_call | solution.py:78
  163.9 11.5 %collective-permute-done.30.q_ref = bf16[256,1280]{1,0:T(8,128)(2,1)} collective-permute-done((bf16[256,1280]{1,0:T(8,128)(2,1)}, bf16[256,1280]{1,0:T(8,128)(2,1)}, u32[]{:S(2)}, u32[]{:S(2)}) %collective-permute-start.30) | collective-permute-done | bytes 655392 | tf_op jit(solution)/shard_map/ppermute | solution.py:177
  177.1 8.6 %shard_map.120 = (bf16[1280,256]{1,0:T(8,128)(2,1)}, f32[2,10,256]{2,1,0:T(8,128)}) custom-call(s32[3]{0:T(128)} %pad_add_fusion.fsel_ref, s32[2]{0:T(128)} %pad_add_fusion.4.rs_ref, bf16[256,1280]{1,0:T(8,128)(2,1)} %collective-permute-done.30.q_ref, bf16[3,128,1280]{2,1,0:T(8,128)(2,1)} %get-tuple-element.300.kf0_ref.kf1_ref, ...), custom_call_target="tpu_custom_call" | custom-call | tf_op jit(solution)/shard_map/pallas_call | solution.py:78
  190.8 8.6 %shard_map.112 = (bf16[1280,256]{1,0:T(8,128)(2,1)}, f32[2,10,256]{2,1,0:T(8,128)}) custom-call(s32[3]{0:T(128)} %pad_add_fusion.fsel_ref, s32[2]{0:T(128)} %pad_add_fusion.4.rs_ref, bf16[256,1280]{1,0:T(8,128)(2,1)} %collective-permute-done.9.q_ref, bf16[3,128,1280]{2,1,0:T(8,128)(2,1)} %get-tuple-element.301.kf0_ref.kf1_ref, ...), custom_call_target="tpu_custom_call" | custom-call | tf_op jit(solution)/shard_map/pallas_call | solution.py:78
  203.3 10.4 %collective-permute-done.33.q_ref = bf16[256,1280]{1,0:T(8,128)(2,1)} collective-permute-done((bf16[256,1280]{1,0:T(8,128)(2,1)}, bf16[256,1280]{1,0:T(8,128)(2,1)}, u32[]{:S(2)}, u32[]{:S(2)}) %collective-permute-start.33) | collective-permute-done | bytes 655392 | tf_op jit(solution)/shard_map/ppermute | solution.py:177
  215.1 8.6 %shard_map.121 = (bf16[1280,256]{1,0:T(8,128)(2,1)}, f32[2,10,256]{2,1,0:T(8,128)}) custom-call(s32[3]{0:T(128)} %pad_add_fusion.fsel_ref, s32[2]{0:T(128)} %pad_add_fusion.3.rs_ref, bf16[256,1280]{1,0:T(8,128)(2,1)} %collective-permute-done.33.q_ref, bf16[3,128,1280]{2,1,0:T(8,128)(2,1)} %get-tuple-element.300.kf0_ref.kf1_ref, ...), custom_call_target="tpu_custom_call" | custom-call | tf_op jit(solution)/shard_map/pallas_call | solution.py:78
  227.9 8.6 %shard_map.113 = (bf16[1280,256]{1,0:T(8,128)(2,1)}, f32[2,10,256]{2,1,0:T(8,128)}) custom-call(s32[3]{0:T(128)} %pad_add_fusion.fsel_ref, s32[2]{0:T(128)} %pad_add_fusion.5.rs_ref, bf16[256,1280]{1,0:T(8,128)(2,1)} %collective-permute-done.12.q_ref, bf16[3,128,1280]{2,1,0:T(8,128)(2,1)} %get-tuple-element.301.kf0_ref.kf1_ref, ...), custom_call_target="tpu_custom_call" | custom-call | tf_op jit(solution)/shard_map/pallas_call | solution.py:78
  241.6 8.5 %collective-permute-done.36.q_ref = bf16[256,1280]{1,0:T(8,128)(2,1)} collective-permute-done((bf16[256,1280]{1,0:T(8,128)(2,1)}, bf16[256,1280]{1,0:T(8,128)(2,1)}, u32[]{:S(2)}, u32[]{:S(2)}) %collective-permute-start.36) | collective-permute-done | bytes 655392 | tf_op jit(solution)/shard_map/ppermute | solution.py:177
  251.5 8.6 %shard_map.122 = (bf16[1280,256]{1,0:T(8,128)(2,1)}, f32[2,10,256]{2,1,0:T(8,128)}) custom-call(s32[3]{0:T(128)} %pad_add_fusion.fsel_ref, s32[2]{0:T(128)} %pad_add_fusion.2.rs_ref, bf16[256,1280]{1,0:T(8,128)(2,1)} %collective-permute-done.36.q_ref, bf16[3,128,1280]{2,1,0:T(8,128)(2,1)} %get-tuple-element.300.kf0_ref.kf1_ref, ...), custom_call_target="tpu_custom_call" | custom-call | tf_op jit(solution)/shard_map/pallas_call | solution.py:78
  264.2 8.6 %shard_map.114 = (bf16[1280,256]{1,0:T(8,128)(2,1)}, f32[2,10,256]{2,1,0:T(8,128)}) custom-call(s32[3]{0:T(128)} %pad_add_fusion.fsel_ref, s32[2]{0:T(128)} %pad_add_fusion.6.rs_ref, bf16[256,1280]{1,0:T(8,128)(2,1)} %collective-permute-done.15.q_ref, bf16[3,128,1280]{2,1,0:T(8,128)(2,1)} %get-tuple-element.301.kf0_ref.kf1_ref, ...), custom_call_target="tpu_custom_call" | custom-call | tf_op jit(solution)/shard_map/pallas_call | solution.py:78
  286.0 8.6 %shard_map.123 = (bf16[1280,256]{1,0:T(8,128)(2,1)}, f32[2,10,256]{2,1,0:T(8,128)}) custom-call(s32[3]{0:T(128)} %pad_add_fusion.fsel_ref, s32[2]{0:T(128)} %pad_add_fusion.1.rs_ref, bf16[256,1280]{1,0:T(8,128)(2,1)} %collective-permute-done.39.q_ref, bf16[3,128,1280]{2,1,0:T(8,128)(2,1)} %get-tuple-element.300.kf0_ref.kf1_ref, ...), custom_call_target="tpu_custom_call" | custom-call | tf_op jit(solution)/shard_map/pallas_call | solution.py:78
  298.5 8.6 %shard_map.115 = (bf16[1280,256]{1,0:T(8,128)(2,1)}, f32[2,10,256]{2,1,0:T(8,128)}) custom-call(s32[3]{0:T(128)} %pad_add_fusion.fsel_ref, s32[2]{0:T(128)} %pad_add_fusion.7.rs_ref, bf16[256,1280]{1,0:T(8,128)(2,1)} %collective-permute-done.18.q_ref, bf16[3,128,1280]{2,1,0:T(8,128)(2,1)} %get-tuple-element.301.kf0_ref.kf1_ref, ...), custom_call_target="tpu_custom_call" | custom-call | tf_op jit(solution)/shard_map/pallas_call | solution.py:78
  311.9 8.4 %collective-permute-done.20 = f32[2,10,256]{2,1,0:T(8,128)S(1)} collective-permute-done((f32[2,10,256]{2,1,0:T(8,128)S(1)}, f32[2,10,256]{2,1,0:T(8,128)S(1)}, u32[]{:S(2)}, u32[]{:S(2)}) %collective-permute-start.20) | collective-permute-done | bytes 20512 | tf_op jit(solution)/shard_map/ppermute | solution.py:185
  324.1 12.8 %convolution_convert_fusion = bf16[192,5120]{1,0:T(8,128)(2,1)} fusion(bf16[2560,5120]{1,0:T(8,128)(2,1)} %param.19, bf16[2560,256]{1,0:T(8,128)(2,1)S(1)} %fusion.1, s32[]{:T(128)S(6)} %select_n.261), kind=kOutput, calls=%fused_computation.1 | convolution fusion | flops 5034147840 | bytes 29491204 | tf_op jit(solution)/shard_map/dot_general | solution.py:204
  348.9 7.2 %shard_map.140 = (bf16[1280,128]{1,0:T(8,128)(2,1)}, f32[2,10,128]{2,1,0:T(8,128)}) custom-call(s32[3]{0:T(128)} %pad_add_fusion.fsel_ref, s32[2]{0:T(128)} %pad_add_fusion.8.rs_ref, bf16[128,1280]{1,0:T(8,128)(2,1)} %copy-done.3, bf16[3,128,1280]{2,1,0:T(8,128)(2,1)} %get-tuple-element.300.kf0_ref.kf1_ref, ...), custom_call_target="tpu_custom_call" | custom-call | tf_op jit(solution)/shard_map/pallas_call | solution.py:78
  356.1 7.2 %shard_map.132 = (bf16[1280,128]{1,0:T(8,128)(2,1)}, f32[2,10,128]{2,1,0:T(8,128)}) custom-call(s32[3]{0:T(128)} %pad_add_fusion.fsel_ref, s32[2]{0:T(128)} %pad_add_fusion.8.rs_ref, bf16[128,1280]{1,0:T(8,128)(2,1)} %get-tuple-element.217.q_ref, bf16[3,128,1280]{2,1,0:T(8,128)(2,1)} %get-tuple-element.301.kf0_ref.kf1_ref, ...), custom_call_target="tpu_custom_call" | custom-call | tf_op jit(solution)/shard_map/pallas_call | solution.py:78
  363.3 7.2 %shard_map.125 = (bf16[1280,128]{1,0:T(8,128)(2,1)}, f32[2,10,128]{2,1,0:T(8,128)}) custom-call(s32[3]{0:T(128)} %pad_add_fusion.fsel_ref, s32[2]{0:T(128)} %pad_add_fusion.1.rs_ref, bf16[128,1280]{1,0:T(8,128)(2,1)} %collective-permute-done.42.q_ref, bf16[3,128,1280]{2,1,0:T(8,128)(2,1)} %get-tuple-element.301.kf0_ref.kf1_ref, ...), custom_call_target="tpu_custom_call" | custom-call | tf_op jit(solution)/shard_map/pallas_call | solution.py:78
  389.6 7.2 %shard_map.126 = (bf16[1280,128]{1,0:T(8,128)(2,1)}, f32[2,10,128]{2,1,0:T(8,128)}) custom-call(s32[3]{0:T(128)} %pad_add_fusion.fsel_ref, s32[2]{0:T(128)} %pad_add_fusion.2.rs_ref, bf16[128,1280]{1,0:T(8,128)(2,1)} %copy-done.20, bf16[3,128,1280]{2,1,0:T(8,128)(2,1)} %get-tuple-element.301.kf0_ref.kf1_ref, ...), custom_call_target="tpu_custom_call" | custom-call | tf_op jit(solution)/shard_map/pallas_call | solution.py:78
  405.5 7.2 %shard_map.135 = (bf16[1280,128]{1,0:T(8,128)(2,1)}, f32[2,10,128]{2,1,0:T(8,128)}) custom-call(s32[3]{0:T(128)} %pad_add_fusion.fsel_ref, s32[2]{0:T(128)} %pad_add_fusion.5.rs_ref, bf16[128,1280]{1,0:T(8,128)(2,1)} %copy-done.12, bf16[3,128,1280]{2,1,0:T(8,128)(2,1)} %get-tuple-element.300.kf0_ref.kf1_ref, ...), custom_call_target="tpu_custom_call" | custom-call | tf_op jit(solution)/shard_map/pallas_call | solution.py:78
  437.3 7.2 %shard_map.136 = (bf16[1280,128]{1,0:T(8,128)(2,1)}, f32[2,10,128]{2,1,0:T(8,128)}) custom-call(s32[3]{0:T(128)} %pad_add_fusion.fsel_ref, s32[2]{0:T(128)} %pad_add_fusion.4.rs_ref, bf16[128,1280]{1,0:T(8,128)(2,1)} %copy-done.10, bf16[3,128,1280]{2,1,0:T(8,128)(2,1)} %get-tuple-element.300.kf0_ref.kf1_ref, ...), custom_call_target="tpu_custom_call" | custom-call | tf_op jit(solution)/shard_map/pallas_call | solution.py:78
  480.2 7.3 %collective-permute-done.54.q_ref = bf16[128,1280]{1,0:T(8,128)(2,1)S(1)} collective-permute-done((bf16[128,1280]{1,0:T(8,128)(2,1)S(1)}, bf16[128,1280]{1,0:T(8,128)(2,1)S(1)}, u32[]{:S(2)}, u32[]{:S(2)}) %collective-permute-start.54) | collective-permute-done | bytes 327712 | tf_op jit(solution)/shard_map/ppermute | solution.py:177
  504.6 7.2 %shard_map.138 = (bf16[1280,128]{1,0:T(8,128)(2,1)}, f32[2,10,128]{2,1,0:T(8,128)}) custom-call(s32[3]{0:T(128)} %pad_add_fusion.fsel_ref, s32[2]{0:T(128)} %pad_add_fusion.2.rs_ref, bf16[128,1280]{1,0:T(8,128)(2,1)} %copy-done.8, bf16[3,128,1280]{2,1,0:T(8,128)(2,1)} %get-tuple-element.300.kf0_ref.kf1_ref, ...), custom_call_target="tpu_custom_call" | custom-call | tf_op jit(solution)/shard_map/pallas_call | solution.py:78
  551.8 7.2 %shard_map.131 = (bf16[1280,128]{1,0:T(8,128)(2,1)}, f32[2,10,128]{2,1,0:T(8,128)}) custom-call(s32[3]{0:T(128)} %pad_add_fusion.fsel_ref, s32[2]{0:T(128)} %pad_add_fusion.7.rs_ref, bf16[128,1280]{1,0:T(8,128)(2,1)} %copy-done.26, bf16[3,128,1280]{2,1,0:T(8,128)(2,1)} %get-tuple-element.301.kf0_ref.kf1_ref, ...), custom_call_target="tpu_custom_call" | custom-call | tf_op jit(solution)/shard_map/pallas_call | solution.py:78
  572.4 13.6 %add_convert_fusion = bf16[192,5120]{1,0:T(8,128)(2,1)} fusion(bf16[192,5120]{1,0:T(8,128)(2,1)} %collective-permute-done.84, bf16[2560,5120]{1,0:T(8,128)(2,1)} %param.19, bf16[2560,384]{1,0:T(8,128)(2,1)S(1)} %constant_dynamic-update-slice_fusion, s32[]{:T(128)S(6)} %select_n.260), kind=kOutput, calls=%fused_computation.4 | convolution fusion | flops 5038080000 | bytes 31457284 | tf_op jit(solution)/shard_map/dot_general | solution.py:214
  (433 shorter events, 285.4 us)
Async XLA Ops:
  1.6 47.5 %collective-permute-start.21 = (bf16[256,1280]{1,0:T(8,128)(2,1)S(1)}, bf16[256,1280]{1,0:T(8,128)(2,1)}, u32[]{:S(2)}, u32[]{:S(2)}) collective-permute-start(bf16[256,1280]{1,0:T(8,128)(2,1)S(1)} %get-tuple-element.216.q_ref), channel_id=1, source_target_pairs={{0,4},{8,0},{16,8},{24,16},{28,24},{20,28},{12,20},{4,12},{1,5},{9... | collective-permute-start | bytes 1966088 | tf_op jit(solution)/shard_map/ppermute | solution.py:177
  4.6 62.5 %collective-permute-start = (bf16[256,1280]{1,0:T(8,128)(2,1)S(1)}, bf16[256,1280]{1,0:T(8,128)(2,1)}, u32[]{:S(2)}, u32[]{:S(2)}) collective-permute-start(bf16[256,1280]{1,0:T(8,128)(2,1)S(1)} %get-tuple-element.215.q_ref), channel_id=1, source_target_pairs={{0,8},{8,16},{16,24},{24,28},{28,20},{20,12},{12,4},{4,0},{1,9},{9... | collective-permute-start | bytes 1966088 | tf_op jit(solution)/shard_map/ppermute | solution.py:177
  49.0 46.7 %collective-permute-start.24 = (bf16[256,1280]{1,0:T(8,128)(2,1)}, bf16[256,1280]{1,0:T(8,128)(2,1)}, u32[]{:S(2)}, u32[]{:S(2)}) collective-permute-start(bf16[256,1280]{1,0:T(8,128)(2,1)} %collective-permute-done.21.q_ref), channel_id=1, source_target_pairs={{0,4},{8,0},{16,8},{24,16},{28,24},{20,28},{12,20},{4,12},{1,5},{9... | collective-permute-start | bytes 1966088 | tf_op jit(solution)/shard_map/ppermute | solution.py:177
  62.8 42.5 %collective-permute-start.22 = (bf16[1280,256]{1,0:T(8,128)(2,1)}, bf16[1280,256]{1,0:T(8,128)(2,1)S(1)}, u32[]{:S(2)}, u32[]{:S(2)}) collective-permute-start(bf16[1280,256]{1,0:T(8,128)(2,1)} %get-tuple-element.93), channel_id=1, source_target_pairs={{0,4},{8,0},{16,8},{24,16},{28,24},{20,28},{12,20},{4,12},{1,5},{9... | collective-permute-start | bytes 1966088 | tf_op jit(solution)/shard_map/ppermute | solution.py:178
  65.5 39.0 %collective-permute-start.23 = (f32[2,10,256]{2,1,0:T(8,128)S(1)}, f32[2,10,256]{2,1,0:T(8,128)S(1)}, u32[]{:S(2)}, u32[]{:S(2)}) collective-permute-start(f32[2,10,256]{2,1,0:T(8,128)S(1)} %copy-done.60), channel_id=1, source_target_pairs={{0,4},{8,0},{16,8},{24,16},{28,24},{20,28},{12,20},{4,12},{1,5},{9... | collective-permute-start | bytes 61448 | tf_op jit(solution)/shard_map/ppermute | solution.py:178
  67.1 43.1 %collective-permute-start.3 = (bf16[256,1280]{1,0:T(8,128)(2,1)}, bf16[256,1280]{1,0:T(8,128)(2,1)}, u32[]{:S(2)}, u32[]{:S(2)}) collective-permute-start(bf16[256,1280]{1,0:T(8,128)(2,1)} %collective-permute-done.q_ref), channel_id=1, source_target_pairs={{0,8},{8,16},{16,24},{24,28},{28,20},{20,12},{12,4},{4,0},{1,9},{9... | collective-permute-start | bytes 1966088 | tf_op jit(solution)/shard_map/ppermute | solution.py:177
  106.6 40.2 %collective-permute-start.25 = (bf16[1280,256]{1,0:T(8,128)(2,1)S(1)}, bf16[1280,256]{1,0:T(8,128)(2,1)S(1)}, u32[]{:S(2)}, u32[]{:S(2)}) collective-permute-start(bf16[1280,256]{1,0:T(8,128)(2,1)S(1)} %fusion.15), channel_id=1, source_target_pairs={{0,4},{8,0},{16,8},{24,16},{28,24},{20,28},{12,20},{4,12},{1,5},{9... | collective-permute-start | bytes 1966088 | tf_op jit(solution)/shard_map/ppermute | solution.py:178
  110.2 35.8 %collective-permute-start.26 = (f32[2,10,256]{2,1,0:T(8,128)S(1)}, f32[2,10,256]{2,1,0:T(8,128)S(1)}, u32[]{:S(2)}, u32[]{:S(2)}) collective-permute-start(f32[2,10,256]{2,1,0:T(8,128)S(1)} %pad_maximum_fusion.6), channel_id=1, source_target_pairs={{0,4},{8,0},{16,8},{24,16},{28,24},{20,28},{12,20},{4,12},{1,5},{9... | collective-permute-start | bytes 61448 | tf_op jit(solution)/shard_map/ppermute | solution.py:178
  122.7 38.9 %collective-permute-start.4 = (bf16[1280,256]{1,0:T(8,128)(2,1)S(1)}, bf16[1280,256]{1,0:T(8,128)(2,1)S(1)}, u32[]{:S(2)}, u32[]{:S(2)}) collective-permute-start(bf16[1280,256]{1,0:T(8,128)(2,1)S(1)} %fusion.28), channel_id=1, source_target_pairs={{0,8},{8,16},{16,24},{24,28},{28,20},{20,12},{12,4},{4,0},{1,9},{9... | collective-permute-start | bytes 1966088 | tf_op jit(solution)/shard_map/ppermute | solution.py:178
  148.2 38.4 %collective-permute-start.28 = (bf16[1280,256]{1,0:T(8,128)(2,1)S(1)}, bf16[1280,256]{1,0:T(8,128)(2,1)S(1)}, u32[]{:S(2)}, u32[]{:S(2)}) collective-permute-start(bf16[1280,256]{1,0:T(8,128)(2,1)S(1)} %fusion.13), channel_id=1, source_target_pairs={{0,4},{8,0},{16,8},{24,16},{28,24},{20,28},{12,20},{4,12},{1,5},{9... | collective-permute-start | bytes 1966088 | tf_op jit(solution)/shard_map/ppermute | solution.py:178
  150.7 35.0 %collective-permute-start.29 = (f32[2,10,256]{2,1,0:T(8,128)S(1)}, f32[2,10,256]{2,1,0:T(8,128)S(1)}, u32[]{:S(2)}, u32[]{:S(2)}) collective-permute-start(f32[2,10,256]{2,1,0:T(8,128)S(1)} %pad_maximum_fusion.7), channel_id=1, source_target_pairs={{0,4},{8,0},{16,8},{24,16},{28,24},{20,28},{12,20},{4,12},{1,5},{9... | collective-permute-start | bytes 61448 | tf_op jit(solution)/shard_map/ppermute | solution.py:178
  162.9 37.3 %collective-permute-start.7 = (bf16[1280,256]{1,0:T(8,128)(2,1)S(1)}, bf16[1280,256]{1,0:T(8,128)(2,1)S(1)}, u32[]{:S(2)}, u32[]{:S(2)}) collective-permute-start(bf16[1280,256]{1,0:T(8,128)(2,1)S(1)} %fusion.26), channel_id=1, source_target_pairs={{0,8},{8,16},{16,24},{24,28},{28,20},{20,12},{12,4},{4,0},{1,9},{9... | collective-permute-start | bytes 1966088 | tf_op jit(solution)/shard_map/ppermute | solution.py:178
  187.9 36.6 %collective-permute-start.31 = (bf16[1280,256]{1,0:T(8,128)(2,1)S(1)}, bf16[1280,256]{1,0:T(8,128)(2,1)S(1)}, u32[]{:S(2)}, u32[]{:S(2)}) collective-permute-start(bf16[1280,256]{1,0:T(8,128)(2,1)S(1)} %fusion.11), channel_id=1, source_target_pairs={{0,4},{8,0},{16,8},{24,16},{28,24},{20,28},{12,20},{4,12},{1,5},{9... | collective-permute-start | bytes 1966088 | tf_op jit(solution)/shard_map/ppermute | solution.py:178
  189.3 34.4 %collective-permute-start.32 = (f32[2,10,256]{2,1,0:T(8,128)S(1)}, f32[2,10,256]{2,1,0:T(8,128)S(1)}, u32[]{:S(2)}, u32[]{:S(2)}) collective-permute-start(f32[2,10,256]{2,1,0:T(8,128)S(1)} %pad_maximum_fusion.8), channel_id=1, source_target_pairs={{0,4},{8,0},{16,8},{24,16},{28,24},{20,28},{12,20},{4,12},{1,5},{9... | collective-permute-start | bytes 61448 | tf_op jit(solution)/shard_map/ppermute | solution.py:178
  201.6 35.8 %collective-permute-start.10 = (bf16[1280,256]{1,0:T(8,128)(2,1)S(1)}, bf16[1280,256]{1,0:T(8,128)(2,1)S(1)}, u32[]{:S(2)}, u32[]{:S(2)}) collective-permute-start(bf16[1280,256]{1,0:T(8,128)(2,1)S(1)} %fusion.24), channel_id=1, source_target_pairs={{0,8},{8,16},{16,24},{24,28},{28,20},{20,12},{12,4},{4,0},{1,9},{9... | collective-permute-start | bytes 1966088 | tf_op jit(solution)/shard_map/ppermute | solution.py:178
  225.9 35.0 %collective-permute-start.34 = (bf16[1280,256]{1,0:T(8,128)(2,1)S(1)}, bf16[1280,256]{1,0:T(8,128)(2,1)S(1)}, u32[]{:S(2)}, u32[]{:S(2)}) collective-permute-start(bf16[1280,256]{1,0:T(8,128)(2,1)S(1)} %fusion.9), channel_id=1, source_target_pairs={{0,4},{8,0},{16,8},{24,16},{28,24},{20,28},{12,20},{4,12},{1,5},{9... | collective-permute-start | bytes 1966088 | tf_op jit(solution)/shard_map/ppermute | solution.py:178
  226.9 33.2 %collective-permute-start.35 = (f32[2,10,256]{2,1,0:T(8,128)S(1)}, f32[2,10,256]{2,1,0:T(8,128)S(1)}, u32[]{:S(2)}, u32[]{:S(2)}) collective-permute-start(f32[2,10,256]{2,1,0:T(8,128)S(1)} %pad_maximum_fusion.9), channel_id=1, source_target_pairs={{0,4},{8,0},{16,8},{24,16},{28,24},{20,28},{12,20},{4,12},{1,5},{9... | collective-permute-start | bytes 61448 | tf_op jit(solution)/shard_map/ppermute | solution.py:178
  238.7 34.9 %collective-permute-start.13 = (bf16[1280,256]{1,0:T(8,128)(2,1)S(1)}, bf16[1280,256]{1,0:T(8,128)(2,1)S(1)}, u32[]{:S(2)}, u32[]{:S(2)}) collective-permute-start(bf16[1280,256]{1,0:T(8,128)(2,1)S(1)} %fusion.22), channel_id=1, source_target_pairs={{0,8},{8,16},{16,24},{24,28},{28,20},{20,12},{12,4},{4,0},{1,9},{9... | collective-permute-start | bytes 1966088 | tf_op jit(solution)/shard_map/ppermute | solution.py:178
  262.2 33.2 %collective-permute-start.37 = (bf16[1280,256]{1,0:T(8,128)(2,1)S(1)}, bf16[1280,256]{1,0:T(8,128)(2,1)S(1)}, u32[]{:S(2)}, u32[]{:S(2)}) collective-permute-start(bf16[1280,256]{1,0:T(8,128)(2,1)S(1)} %fusion.7), channel_id=1, source_target_pairs={{0,4},{8,0},{16,8},{24,16},{28,24},{20,28},{12,20},{4,12},{1,5},{9... | collective-permute-start | bytes 1966088 | tf_op jit(solution)/shard_map/ppermute | solution.py:178
  263.8 30.8 %collective-permute-start.38 = (f32[2,10,256]{2,1,0:T(8,128)S(1)}, f32[2,10,256]{2,1,0:T(8,128)S(1)}, u32[]{:S(2)}, u32[]{:S(2)}) collective-permute-start(f32[2,10,256]{2,1,0:T(8,128)S(1)} %pad_maximum_fusion.10), channel_id=1, source_target_pairs={{0,4},{8,0},{16,8},{24,16},{28,24},{20,28},{12,20},{4,12},{1,5},{9... | collective-permute-start | bytes 61448 | tf_op jit(solution)/shard_map/ppermute | solution.py:178
  274.9 33.0 %collective-permute-start.16 = (bf16[1280,256]{1,0:T(8,128)(2,1)S(1)}, bf16[1280,256]{1,0:T(8,128)(2,1)S(1)}, u32[]{:S(2)}, u32[]{:S(2)}) collective-permute-start(bf16[1280,256]{1,0:T(8,128)(2,1)S(1)} %fusion.20), channel_id=1, source_target_pairs={{0,8},{8,16},{16,24},{24,28},{28,20},{20,12},{12,4},{4,0},{1,9},{9... | collective-permute-start | bytes 1966088 | tf_op jit(solution)/shard_map/ppermute | solution.py:178
  336.9 235.5 %collective-permute-start.84 = (bf16[192,5120]{1,0:T(8,128)(2,1)}, bf16[192,5120]{1,0:T(8,128)(2,1)}, u32[]{:S(2)}, u32[]{:S(2)}) collective-permute-start(bf16[192,5120]{1,0:T(8,128)(2,1)} %convolution_convert_fusion), channel_id=1, source_target_pairs={{0,2},{2,0},{1,3},{3,1},{4,6},{6,4},{5,7},{7,5},{8,10},{10,8},{9,1... | collective-permute-start | bytes 5898248 | tf_op jit(solution)/shard_map/ppermute | solution.py:205
  347.2 34.2 %collective-permute-start.65 = (f32[2,10,128]{2,1,0:T(8,128)}, f32[2,10,128]{2,1,0:T(8,128)S(1)}, u32[]{:S(2)}, u32[]{:S(2)}) collective-permute-start(f32[2,10,128]{2,1,0:T(8,128)} %get-tuple-element.128), channel_id=1, source_target_pairs={{0,4},{8,0},{16,8},{24,16},{28,24},{20,28},{12,20},{4,12},{1,5},{9... | collective-permute-start | bytes 30728 | tf_op jit(solution)/shard_map/ppermute | solution.py:178
  404.2 29.3 %collective-permute-start.46 = (bf16[1280,128]{1,0:T(8,128)(2,1)}, bf16[1280,128]{1,0:T(8,128)(2,1)}, u32[]{:S(2)}, u32[]{:S(2)}) collective-permute-start(bf16[1280,128]{1,0:T(8,128)(2,1)} %fusion.56), channel_id=1, source_target_pairs={{0,8},{8,16},{16,24},{24,28},{28,20},{20,12},{12,4},{4,0},{1,9},{9... | collective-permute-start | bytes 983048 | tf_op jit(solution)/shard_map/ppermute | solution.py:178
  430.5 30.8 %collective-permute-start.50 = (f32[2,10,128]{2,1,0:T(8,128)S(1)}, f32[2,10,128]{2,1,0:T(8,128)S(1)}, u32[]{:S(2)}, u32[]{:S(2)}) collective-permute-start(f32[2,10,128]{2,1,0:T(8,128)S(1)} %pad_maximum_fusion.14), channel_id=1, source_target_pairs={{0,8},{8,16},{16,24},{24,28},{28,20},{20,12},{12,4},{4,0},{1,9},{9... | collective-permute-start | bytes 30728 | tf_op jit(solution)/shard_map/ppermute | solution.py:178
  433.4 30.9 %collective-permute-start.70 = (bf16[1280,128]{1,0:T(8,128)(2,1)}, bf16[1280,128]{1,0:T(8,128)(2,1)}, u32[]{:S(2)}, u32[]{:S(2)}) collective-permute-start(bf16[1280,128]{1,0:T(8,128)(2,1)} %fusion.41), channel_id=1, source_target_pairs={{0,4},{8,0},{16,8},{24,16},{28,24},{20,28},{12,20},{4,12},{1,5},{9... | collective-permute-start | bytes 983048 | tf_op jit(solution)/shard_map/ppermute | solution.py:178
  436.5 30.1 %collective-permute-start.49 = (bf16[1280,128]{1,0:T(8,128)(2,1)}, bf16[1280,128]{1,0:T(8,128)(2,1)}, u32[]{:S(2)}, u32[]{:S(2)}) collective-permute-start(bf16[1280,128]{1,0:T(8,128)(2,1)} %fusion.54), channel_id=1, source_target_pairs={{0,8},{8,16},{16,24},{24,28},{28,20},{20,12},{12,4},{4,0},{1,9},{9... | collective-permute-start | bytes 983048 | tf_op jit(solution)/shard_map/ppermute | solution.py:178
  464.3 31.5 %collective-permute-start.53 = (f32[2,10,128]{2,1,0:T(8,128)S(1)}, f32[2,10,128]{2,1,0:T(8,128)S(1)}, u32[]{:S(2)}, u32[]{:S(2)}) collective-permute-start(f32[2,10,128]{2,1,0:T(8,128)S(1)} %pad_maximum_fusion.15), channel_id=1, source_target_pairs={{0,8},{8,16},{16,24},{24,28},{28,20},{20,12},{12,4},{4,0},{1,9},{9... | collective-permute-start | bytes 30728 | tf_op jit(solution)/shard_map/ppermute | solution.py:178
  466.7 32.2 %collective-permute-start.73 = (bf16[1280,128]{1,0:T(8,128)(2,1)}, bf16[1280,128]{1,0:T(8,128)(2,1)}, u32[]{:S(2)}, u32[]{:S(2)}) collective-permute-start(bf16[1280,128]{1,0:T(8,128)(2,1)} %fusion.39), channel_id=1, source_target_pairs={{0,4},{8,0},{16,8},{24,16},{28,24},{20,28},{12,20},{4,12},{1,5},{9... | collective-permute-start | bytes 983048 | tf_op jit(solution)/shard_map/ppermute | solution.py:178
  470.1 30.5 %collective-permute-start.52 = (bf16[1280,128]{1,0:T(8,128)(2,1)}, bf16[1280,128]{1,0:T(8,128)(2,1)}, u32[]{:S(2)}, u32[]{:S(2)}) collective-permute-start(bf16[1280,128]{1,0:T(8,128)(2,1)} %fusion.52), channel_id=1, source_target_pairs={{0,8},{8,16},{16,24},{24,28},{28,20},{20,12},{12,4},{4,0},{1,9},{9... | collective-permute-start | bytes 983048 | tf_op jit(solution)/shard_map/ppermute | solution.py:178
  500.6 29.7 %collective-permute-start.76 = (bf16[1280,128]{1,0:T(8,128)(2,1)S(1)}, bf16[1280,128]{1,0:T(8,128)(2,1)}, u32[]{:S(2)}, u32[]{:S(2)}) collective-permute-start(bf16[1280,128]{1,0:T(8,128)(2,1)S(1)} %fusion.37), channel_id=1, source_target_pairs={{0,4},{8,0},{16,8},{24,16},{28,24},{20,28},{12,20},{4,12},{1,5},{9... | collective-permute-start | bytes 983048 | tf_op jit(solution)/shard_map/ppermute | solution.py:178
  503.9 29.1 %collective-permute-start.55 = (bf16[1280,128]{1,0:T(8,128)(2,1)}, bf16[1280,128]{1,0:T(8,128)(2,1)}, u32[]{:S(2)}, u32[]{:S(2)}) collective-permute-start(bf16[1280,128]{1,0:T(8,128)(2,1)} %fusion.50), channel_id=1, source_target_pairs={{0,8},{8,16},{16,24},{24,28},{28,20},{20,12},{12,4},{4,0},{1,9},{9... | collective-permute-start | bytes 983048 | tf_op jit(solution)/shard_map/ppermute | solution.py:178
  (115 other events, 1539.6 us)
